TPU v7x, 512 devices: a whole 4x8x8 slice. The times are simulated.
512 devices in a mesh: dp: 16 (over y, core), expert: 32 (over x, z).
Axes of the slice: x: 4, y: 8, z: 8, core: 2. Of those that a mesh axis runs over, the one named last changes fastest.
Arguments:
- tokens: bfloat16 [65536, 1024], P(('dp', 'expert')), may hold values from -6 to 6
- routes: int32 [65536, 4], P(('dp', 'expert')), may hold values from 0 to 31, all different within a row; in each aligned block of 128 rows (0 to 127, 128 to 255, ...) at most 32 rows name the same one
- gates: float32 [65536, 4], P(('dp', 'expert')), may hold values from 0.05 to 0.5
- w_in: bfloat16 [32, 1024, 768], P('expert', 'dp'), may hold values from -6 to 6
- w_down: bfloat16 [32, 384, 1024], P('expert', 'dp'), may hold values from -6 to 6
- out_grad: bfloat16 [65536, 1024], P(('dp', 'expert')), may hold values from -6 to 6
Outputs:
- moe_out: bfloat16 [65536, 1024], P(('dp', 'expert'))
- token_grad: bfloat16 [65536, 1024], P(('dp', 'expert'))
- new_w_in: bfloat16 [32, 1024, 768], P('expert', 'dp')
- new_w_down: bfloat16 [32, 384, 1024], P('expert', 'dp')
Inputs may be any that keep to these rules, and one draw needn't show every extreme that they name: `routes`: within one device's 128 tokens no expert is named more than 32 times, a bound that some block reaches; a token names 4 different experts.
All inputs are finite; a program needn't handle non-finite values.
Results may differ from a plain program's by a relative error of at most 0.014.
Values may be sent and summed in bfloat16 or wider, within the bound.
No kernel may reach another device: no remote copies, remote signals or barrier semaphores. Data moves between devices by JAX's collectives and lax.ppermute only.
A program may use at most 64 MiB of HBM per device.

v0:
```python
import jax
import jax.numpy as jnp
from jax import lax
from jax.sharding import PartitionSpec as P

step_rate = 0.5


def slot_numbers(route_rows, experts, capacity):
    flat_routes = route_rows.reshape(-1)
    one_hot = (flat_routes[:, None] == jnp.arange(experts, dtype=jnp.int32)[None, :]).astype(
        jnp.int32
    )
    running = jnp.cumsum(one_hot, axis=0)
    position = jnp.sum(one_hot * running, axis=1) - 1
    return flat_routes * capacity + position


def expert_forward(inputs, full_in, full_down):
    model_width = full_in.shape[1]
    hidden_units = full_down.shape[1]
    projected = jnp.einsum(
        "sxcd,xdj->sxcj", inputs, full_in, preferred_element_type=jnp.float32
    ) * model_width ** (-0.5)
    gate_part = projected[..., :hidden_units]
    up_part = projected[..., hidden_units:]
    activation = (jax.nn.silu(gate_part) * up_part).astype(jnp.bfloat16)
    results = (
        jnp.einsum("sxcf,xfd->sxcd", activation, full_down, preferred_element_type=jnp.float32)
        * hidden_units ** (-0.5)
    ).astype(jnp.bfloat16)
    return (projected, activation, results)


def expert_backward(projected, grad_rows, full_in, full_down):
    model_width = full_in.shape[1]
    hidden_units = full_down.shape[1]
    grad_act = jnp.einsum(
        "sxcd,xfd->sxcf", grad_rows, full_down, preferred_element_type=jnp.float32
    ) * hidden_units ** (-0.5)
    gate_part = projected[..., :hidden_units]
    up_part = projected[..., hidden_units:]
    sigmoid_gate = jax.nn.sigmoid(gate_part)
    grad_gate = grad_act * up_part * sigmoid_gate * (1.0 + gate_part * (1.0 - sigmoid_gate))
    grad_up = grad_act * jax.nn.silu(gate_part)
    grad_hidden = jnp.concatenate([grad_gate, grad_up], axis=-1).astype(jnp.bfloat16)
    grad_inputs = (
        jnp.einsum("sxcj,xdj->sxcd", grad_hidden, full_in, preferred_element_type=jnp.float32)
        * model_width ** (-0.5)
    ).astype(jnp.bfloat16)
    return (grad_hidden, grad_inputs)


def body(tokens, routes, gates, w_in, w_down, out_grad):
    tok_rows, model_width = tokens.shape
    top_count = routes.shape[1]
    per_device = w_in.shape[0]
    hidden_units = w_down.shape[2] and w_in.shape[2] // 2
    sources = lax.axis_size("expert")
    experts = per_device * sources
    capacity = min(tok_rows, 2 * tok_rows * top_count // experts)
    slot_index = slot_numbers(routes, experts, capacity)
    token_of = jnp.arange(tok_rows * top_count, dtype=jnp.int32) // top_count
    layout = (sources, per_device, capacity, model_width)
    send_inputs = (
        jnp.zeros((experts * capacity, model_width), jnp.bfloat16)
        .at[slot_index]
        .set(tokens[token_of])
        .reshape(layout)
    )
    scaled = (gates.reshape(-1)[:, None] * out_grad[token_of].astype(jnp.float32)).astype(
        jnp.bfloat16
    )
    send_grads = (
        jnp.zeros((experts * capacity, model_width), jnp.bfloat16)
        .at[slot_index]
        .set(scaled)
        .reshape(layout)
    )
    full_in, full_down = (
        lax.all_gather(w_in, "dp", axis=1, tiled=True),
        lax.all_gather(w_down, "dp", axis=1, tiled=True),
    )
    inputs_here = lax.all_to_all(send_inputs, "expert", split_axis=0, concat_axis=0, tiled=True)
    projected_here, activation_here, results_here = expert_forward(inputs_here, full_in, full_down)
    results_home = lax.all_to_all(results_here, "expert", split_axis=0, concat_axis=0, tiled=True)
    grad_rows = lax.all_to_all(send_grads, "expert", split_axis=0, concat_axis=0, tiled=True)
    grad_hidden, grad_inputs = expert_backward(projected_here, grad_rows, full_in, full_down)
    inputs_back = lax.all_to_all(grad_inputs, "expert", split_axis=0, concat_axis=0, tiled=True)
    picked = results_home.reshape(experts * capacity, model_width)[slot_index].astype(jnp.float32)
    picked = picked.reshape(tok_rows, top_count, model_width)
    moe_out = jnp.sum(picked * gates[:, :, None], axis=1).astype(jnp.bfloat16)
    back_rows = inputs_back.reshape(experts * capacity, model_width)[slot_index].astype(jnp.float32)
    token_grad = jnp.sum(back_rows.reshape(tok_rows, top_count, model_width), axis=1).astype(
        jnp.bfloat16
    )
    column_part = inputs_here
    summed_in = lax.psum_scatter(
        (
            jnp.einsum(
                "sxcd,sxcj->dxj", column_part, grad_hidden, preferred_element_type=jnp.float32
            )
            * model_width ** (-0.5)
        ).astype(jnp.bfloat16),
        "dp",
        scatter_dimension=0,
        tiled=True,
    ).astype(jnp.float32)
    column_part = activation_here
    summed_down = lax.psum_scatter(
        (
            jnp.einsum("sxcf,sxcd->fxd", column_part, grad_rows, preferred_element_type=jnp.float32)
            * hidden_units ** (-0.5)
        ).astype(jnp.bfloat16),
        "dp",
        scatter_dimension=0,
        tiled=True,
    ).astype(jnp.float32)
    new_w_in = (w_in.astype(jnp.float32) - step_rate * jnp.transpose(summed_in, (1, 0, 2))).astype(
        jnp.bfloat16
    )
    new_w_down = (
        w_down.astype(jnp.float32) - step_rate * jnp.transpose(summed_down, (1, 0, 2))
    ).astype(jnp.bfloat16)
    return (moe_out, token_grad, new_w_in, new_w_down)


def solution(mesh):
    return jax.shard_map(
        body,
        mesh=mesh,
        in_specs=(
            P(("dp", "expert"), None),
            P(("dp", "expert"), None),
            P(("dp", "expert"), None),
            P("expert", "dp", None),
            P("expert", "dp", None),
            P(("dp", "expert"), None),
        ),
        out_specs=(
            P(("dp", "expert"), None),
            P(("dp", "expert"), None),
            P("expert", "dp", None),
            P("expert", "dp", None),
        ),
        check_vma=False,
    )
```

profile of v0, /device:TPU:25, one launch (start us, length us, event | category | flops | bytes accessed | tf_op | source)
XLA Modules:
  0.0 371.1 jit_solution(6107741425047522396)
XLA Ops:
  7.2 0.0 copy-start
  7.2 0.8 copy.34
  8.0 0.1 eq.29
  8.1 0.1 eq.25
  8.2 0.7 broadcast_multiply_fusion
  8.9 1.2 reduce-window.6
  10.1 0.2 slice_reduce_fusion
  10.4 0.1 fusion.51
  10.5 0.1 copy.33
  10.6 0.1 mul.160
  10.7 0.0 copy-done
  10.8 7.7 %scatter_custom_fusion = bf16[1024,1024]{1,0:T(8,128)(2,1)} fusion(s32[512]{0:T(512)S(1)} %bitcast.146, bf16[128,1024]{1,0:T(8,128)(2,1)S(1)} %copy-done, s32[1024]{0:T(1024)S(1)} %pad_clamp_fusion.1, bf16[]{:T(256)} %constant.17.clone.1), kind=kCustom, calls=%fused_computation.41 | custom fusion | bytes 2097154 | tf_op jit(solution)/shard_map/scatter | solution.py:68
  18.5 0.0 copy-start.5
  18.5 13.2 %all-to-all-start = ((bf16[32,1,32,1024]{3,2,1,0:T(8,128)(2,1)}), bf16[32,1,32,1024]{3,2,1,0:T(8,128)(2,1)S(1)}, u32[]{:S(2)}, u32[]{:S(2)}) async-start(bf16[32,1,32,1024]{3,2,1,0:T(8,128)(2,1)} %bitcast.4), calls=%async_computation | async-start | bytes 4194304 | tf_op jit(solution)/shard_map/all_to_all | solution.py:84
  31.7 0.0 copy-done.5
  31.7 0.1 copy.38
  31.8 0.1 mul.173
  31.9 0.0 copy-done.3
  32.0 7.8 %scatter_custom_fusion.1 = bf16[1024,1024]{1,0:T(8,128)(2,1)} fusion(s32[512]{0:T(512)S(1)} %bitcast.147, f32[512]{0:T(512)S(1)} %mul.173, bf16[]{:T(256)} %constant.17.clone.1, bf16[128,1024]{1,0:T(8,128)(2,1)S(1)} %copy-done.3, s32[1024]{0:T(1024)S(1)} %pad_clamp_fusion.1), kind=kCustom, calls=%fused_computation.40 | custom fusion | flops 1572864 | bytes 2365442 | tf_op jit(solution)/shard_map/scatter | solution.py:77
  39.8 40.7 %all-to-all-done = bf16[32,1,32,1024]{3,2,1,0:T(8,128)(2,1)S(1)} async-done(((bf16[32,1,32,1024]{3,2,1,0:T(8,128)(2,1)}), bf16[32,1,32,1024]{3,2,1,0:T(8,128)(2,1)S(1)}, u32[]{:S(2)}, u32[]{:S(2)}) %all-to-all-start) | async-done | bytes 2097184 | tf_op jit(solution)/shard_map/all_to_all | solution.py:84
  80.4 7.3 %all-to-all-start.2 = ((bf16[32,1,32,1024]{3,2,1,0:T(8,128)(2,1)}), bf16[32,1,32,1024]{3,2,1,0:T(8,128)(2,1)}, u32[]{:S(2)}, u32[]{:S(2)}) async-start(bf16[32,1,32,1024]{3,2,1,0:T(8,128)(2,1)} %bitcast.21), calls=%async_computation.2 | async-start | bytes 4194304 | tf_op jit(solution)/shard_map/all_to_all | solution.py:87
  87.7 0.0 all-gather.2.cloned.1.call-start
  87.8 0.7 all-gather.2.cloned.1.call-update
  88.4 0.0 copy-done.4
  88.4 18.9 %all_gather.7 = bf16[1,384,1024]{2,1,0:T(8,128)(2,1)S(1)} all-gather(bf16[1,24,1024]{2,1,0:T(8,128)(2,1)S(1)} %copy-done.4), channel_id=1, replica_groups=mesh['dp'=16,'expert'=32] {'dp'}, dimensions={1}, use_global_device_ids=true | all-gather | bytes 835584 | tf_op jit(solution)/shard_map/all_gather | solution.py:82
  107.4 26.6 %all-gather.2.cloned.1.call-done = bf16[1,1024,768]{2,1,0:T(8,128)(2,1)} async-done(((bf16[1,64,768]{2,1,0:T(8,128)(2,1)}), bf16[1,1024,768]{2,1,0:T(8,128)(2,1)}) %all-gather.2.cloned.1.call-update) | async-done | bytes 1572880 | tf_op jit(solution)/shard_map/all_gather | solution.py:81
  133.9 0.0 copy-done.1
  133.9 4.9 %multiply_bitcast_fusion = f32[32,1,32,768]{3,2,0,1:T(8,128)} fusion(bf16[32,1,32,1024]{3,2,1,0:T(8,128)(2,1)S(1)} %all-to-all-done, bf16[1,1024,768]{2,1,0:T(8,128)(2,1)} %all-gather.2.cloned.1.call-done), kind=kOutput, calls=%fused_computation.10 | convolution fusion | flops 1611399168 | bytes 6815744 | tf_op jit(solution)/shard_map/sxcd,xdj->sxcj/dot_general | solution.py:22
  138.9 0.0 all-to-all-done.2
  138.9 5.3 %fusion.44 = (bf16[32,32,384]{2,1,0:T(8,128)(2,1)S(1)}, bf16[32,32,384]{2,1,0:T(8,128)(2,1)S(1)}, bf16[32,32,384]{2,1,0:T(8,128)(2,1)}) fusion(f32[32,1,32,768]{3,2,0,1:T(8,128)} %multiply_bitcast_fusion, bf16[1,384,1024]{2,1,0:T(8,128)(2,1)S(1)} %all_gather.7, bf16[32,1,32,1024]{3,2,1,0:T(8,128)(2,1)} %all-to-all-done.2), kind=kOutput, calls=%fused_computation.50 | convolution fusion | flops 811597824 | bytes 8388608 | tf_op jit(solution)/shard_map/sxcd,xfd->sxcf/dot_general | solution.py:38
  144.2 0.9 copy-done.7
  145.1 0.2 copy-done.9
  145.4 0.0 copy-done.6
  145.4 3.2 fusion.14
  148.6 9.7 %all-to-all-start.3 = ((bf16[32,1,32,1024]{3,2,1,0:T(8,128)(2,1)}), bf16[32,1,32,1024]{3,2,1,0:T(8,128)(2,1)S(1)}, u32[]{:S(2)}, u32[]{:S(2)}) async-start(bf16[32,1,32,1024]{3,2,1,0:T(8,128)(2,1)} %fusion.14), calls=%async_computation.3 | async-start | bytes 4194304 | tf_op jit(solution)/shard_map/all_to_all | solution.py:89
  158.2 0.0 all-reduce.3.cloned.1.call-start
  158.3 3.9 %fusion.31 = bf16[384,1,1024]{0,2,1:T(8,128)(2,1)} fusion(bf16[32,32,384]{2,1,0:T(8,128)(2,1)} %get-tuple-element.18, bf16[32,1,32,1024]{3,2,1,0:T(8,128)(2,1)} %all-to-all-done.2), kind=kOutput, calls=%fused_computation.39 | convolution fusion | flops 806092800 | bytes 3670016 | tf_op jit(solution)/shard_map/sxcf,sxcd->fxd/dot_general | solution.py:112
  162.2 4.8 %copy.43 = bf16[384,1,1024]{2,1,0:T(2,128)(2,1)} copy(bf16[384,1,1024]{0,2,1:T(8,128)(2,1)} %fusion.31) | data formatting | bytes 1572864 | tf_op jit(solution)/shard_map/convert_element_type | solution.py:114
  167.0 0.0 all-reduce.3.cloned.1.call-update
  167.1 3.7 fusion.13
  170.8 36.4 %all-to-all-done.3 = bf16[32,1,32,1024]{3,2,1,0:T(8,128)(2,1)S(1)} async-done(((bf16[32,1,32,1024]{3,2,1,0:T(8,128)(2,1)}), bf16[32,1,32,1024]{3,2,1,0:T(8,128)(2,1)S(1)}, u32[]{:S(2)}, u32[]{:S(2)}) %all-to-all-start.3) | async-done | bytes 2097184 | tf_op jit(solution)/shard_map/all_to_all | solution.py:89
  207.1 7.6 %all-to-all-start.1 = ((bf16[32,1,32,1024]{3,2,1,0:T(8,128)(2,1)}), bf16[32,1,32,1024]{3,2,1,0:T(8,128)(2,1)}, u32[]{:S(2)}, u32[]{:S(2)}) async-start(bf16[32,1,32,1024]{3,2,1,0:T(8,128)(2,1)} %fusion.13), calls=%async_computation.1 | async-start | bytes 4194304 | tf_op jit(solution)/shard_map/all_to_all | solution.py:86
  214.8 0.0 reduce-scatter.4.cloned.1.call-start
  214.8 0.0 copy-done.8
  214.8 4.8 %fusion.23 = bf16[1024,768]{0,1:T(8,128)(2,1)} fusion(bf16[32,1,32,1024]{3,2,1,0:T(8,128)(2,1)} %copy-done.1, bf16[32,32,384]{2,1,0:T(8,128)(2,1)} %copy-done.9, bf16[32,32,384]{2,1,0:T(8,128)(2,1)S(1)} %copy-done.8), kind=kOutput, calls=%fused_computation.37 | convolution fusion | flops 1615331328 | bytes 5242880 | tf_op jit(solution)/shard_map/sxcd,sxcj->dxj/dot_general | solution.py:100
  219.7 2.6 copy.48
  222.3 0.0 reduce-scatter.4.cloned.1.call-update
  222.3 0.0 copy-done.2
  222.3 0.2 copy.41
  222.5 1.3 dynamic-slice
  224.5 62.4 %all-reduce.3.cloned.1.call-done = bf16[384,1,1024]{2,1,0:T(2,128)(2,1)} async-done(((bf16[384,1,1024]{2,1,0:T(2,128)(2,1)}), bf16[384,1,1024]{2,1,0:T(2,128)(2,1)}) %all-reduce.3.cloned.1.call-update) | async-done | bytes 786448
  286.8 1.0 fusion.49
  287.8 0.6 copy.45
  288.5 62.2 %reduce-scatter.4.cloned.1.call-done = bf16[64,768]{1,0:T(8,128)(2,1)} async-done(((bf16[1024,768]{1,0:T(8,128)(2,1)}), bf16[64,768]{1,0:T(8,128)(2,1)}) %reduce-scatter.4.cloned.1.call-update) | async-done | bytes 98320
  350.7 1.1 copy.49
  351.7 0.1 fusion.45
  351.8 0.8 copy.44
  352.6 2.0 gather_fusion.1
  354.6 0.4 gather.18
  355.1 2.1 reduce_sum.32
  357.2 0.0 all-to-all-done.1
  357.2 4.6 %gather_fusion = bf16[512,1024]{1,0:T(8,128)(2,1)S(1)} fusion(bf16[1024,1024]{1,0:T(8,128)(2,1)} %bitcast.20, s32[1024]{0:T(1024)S(1)} %pad_clamp_fusion), kind=kCustom, calls=%fused_computation.1 | custom fusion | bytes 2099200 | tf_op jit(solution)/shard_map/gather | solution.py:90
  361.8 0.7 reshape.219
  362.5 2.1 multiply_reduce_fusion
  (16 shorter events, 0.1 us)
Async XLA Ops:
  7.2 3.6 copy-start
  18.5 13.2 %copy-start.5 = (f32[128,4]{0,1:T(4,128)S(1)}, f32[128,4]{0,1:T(4,128)}, u32[]{:S(2)}) copy-start(f32[128,4]{0,1:T(4,128)} %param.8) | copy-start | bytes 6148
  18.5 13.4 %copy-start.3 = (bf16[128,1024]{1,0:T(8,128)(2,1)S(1)}, bf16[128,1024]{1,0:T(8,128)(2,1)}, u32[]{:S(2)}) copy-start(bf16[128,1024]{1,0:T(8,128)(2,1)} %param.11) | copy-start | bytes 786436
  18.5 61.9 %all-to-all-start = ((bf16[32,1,32,1024]{3,2,1,0:T(8,128)(2,1)}), bf16[32,1,32,1024]{3,2,1,0:T(8,128)(2,1)S(1)}, u32[]{:S(2)}, u32[]{:S(2)}) async-start(bf16[32,1,32,1024]{3,2,1,0:T(8,128)(2,1)} %bitcast.4), calls=%async_computation | async-start | bytes 4194304 | tf_op jit(solution)/shard_map/all_to_all | solution.py:84
  80.4 53.5 %copy-start.1 = (bf16[32,1,32,1024]{3,2,1,0:T(8,128)(2,1)}, bf16[32,1,32,1024]{3,2,1,0:T(8,128)(2,1)S(1)}, u32[]{:S(2)}) copy-start(bf16[32,1,32,1024]{3,2,1,0:T(8,128)(2,1)S(1)} %all-to-all-done) | copy-start | bytes 6291460
  80.4 8.0 %copy-start.4 = (bf16[1,24,1024]{2,1,0:T(8,128)(2,1)S(1)}, bf16[1,24,1024]{2,1,0:T(8,128)(2,1)}, u32[]{:S(2)}) copy-start(bf16[1,24,1024]{2,1,0:T(8,128)(2,1)} %param.10) | copy-start | bytes 147460
  80.4 58.4 %all-to-all-start.2 = ((bf16[32,1,32,1024]{3,2,1,0:T(8,128)(2,1)}), bf16[32,1,32,1024]{3,2,1,0:T(8,128)(2,1)}, u32[]{:S(2)}, u32[]{:S(2)}) async-start(bf16[32,1,32,1024]{3,2,1,0:T(8,128)(2,1)} %bitcast.21), calls=%async_computation.2 | async-start | bytes 4194304 | tf_op jit(solution)/shard_map/all_to_all | solution.py:87
  87.7 46.2 %all-gather.2.cloned.1.call-start = ((), (), s32[]{:S(2)}) async-start(), calls=%async_computation.5 | async-start | bytes 1671168 | tf_op jit(solution)/shard_map/all_gather | solution.py:81
  138.9 6.5 %copy-start.6 = (bf16[1,1024,768]{2,1,0:T(8,128)(2,1)S(1)}, bf16[1,1024,768]{2,1,0:T(8,128)(2,1)}, u32[]{:S(2)}) copy-start(bf16[1,1024,768]{2,1,0:T(8,128)(2,1)} %all-gather.2.cloned.1.call-done) | copy-start | bytes 4718596
  144.2 0.9 copy-start.7
  144.2 1.2 copy-start.9
  148.6 58.6 %all-to-all-start.3 = ((bf16[32,1,32,1024]{3,2,1,0:T(8,128)(2,1)}), bf16[32,1,32,1024]{3,2,1,0:T(8,128)(2,1)S(1)}, u32[]{:S(2)}, u32[]{:S(2)}) async-start(bf16[32,1,32,1024]{3,2,1,0:T(8,128)(2,1)} %fusion.14), calls=%async_computation.3 | async-start | bytes 4194304 | tf_op jit(solution)/shard_map/all_to_all | solution.py:89
  158.2 128.6 %all-reduce.3.cloned.1.call-start = ((), (), s32[]{:S(2)}) async-start(), calls=%async_computation.7 | async-start | bytes 3145728
  170.8 44.1 %copy-start.8 = (bf16[32,32,384]{2,1,0:T(8,128)(2,1)S(1)}, bf16[32,32,384]{2,1,0:T(8,128)(2,1)}, u32[]{:S(2)}) copy-start(bf16[32,32,384]{2,1,0:T(8,128)(2,1)} %copy-done.7) | copy-start | bytes 2359300
  207.1 150.0 %all-to-all-start.1 = ((bf16[32,1,32,1024]{3,2,1,0:T(8,128)(2,1)}), bf16[32,1,32,1024]{3,2,1,0:T(8,128)(2,1)}, u32[]{:S(2)}, u32[]{:S(2)}) async-start(bf16[32,1,32,1024]{3,2,1,0:T(8,128)(2,1)} %fusion.13), calls=%async_computation.1 | async-start | bytes 4194304 | tf_op jit(solution)/shard_map/all_to_all | solution.py:86
  214.8 135.9 %reduce-scatter.4.cloned.1.call-start = ((), (), s32[]{:S(2)}) async-start(), calls=%async_computation.6 | async-start | bytes 1671168
  219.7 2.7 copy-start.2
Sparse Core Ops, SparseCore 0:
  90.7 43.2 all-gather.1
  167.2 119.5 all-reduce.2
  289.9 60.7 reduce-scatter.3
where the time goes:
time: 372 us; the launch traced here: 371 us
  waiting for transfers between devices  229 us (62%)
  starting transfers between devices  37.9 us (10%)
  local copies, waits for them, and re-layouts  29.8 us (8%)
  matrix products  25.9 us (7%)
  blocking collectives  18.9 us (5%)
  other arithmetic  15.1 us (4%)
  between operations  14.6 us (4%)
    unnamed x5, waiting for transfers between devices  125 us
    all_to_all x1, waiting for transfers between devices, body(): lax.all_to_all(send_inputs, 'expert', split_axis=0, concat_axis=0, tiled=...  40.7 us
    all_to_all x1, waiting for transfers between devices, body(): lax.all_to_all(grad_inputs, 'expert', split_axis=0, concat_axis=0, tiled=...  36.4 us
    all_gather x1, waiting for transfers between devices, body(): lax.all_gather(w_in, 'dp', axis=1, tiled=True)  26.6 us
    all_gather x1, blocking collectives, body(): lax.all_gather(w_down, 'dp', axis=1, tiled=True)  18.9 us
    all_to_all x1, starting transfers between devices, body(): lax.all_to_all(send_inputs, 'expert', split_axis=0, concat_axis=0, tiled=...  13.2 us
    all_to_all x1, starting transfers between devices, body(): lax.all_to_all(grad_inputs, 'expert', split_axis=0, concat_axis=0, tiled=...  9.65 us
    unnamed x28, local copies, waits for them, and re-layouts  8.68 us
  transfers between devices with their start and end apart: 7, of which 5 were waited for; matrix products, arithmetic and copies ran while one was open for 11% of the time, Pallas kernels for 0%

commit v1 on v0

--- a/solution.py
+++ b/solution.py
@@ -4,6 +4,27 @@
 from jax.sharding import PartitionSpec as P
 
 step_rate = 0.5
+
+
+def ring_gather(x, axis, dim):
+    length, mine, rows = (lax.axis_size(axis), lax.axis_index(axis), x.shape[dim])
+    right = [(i, (i + 1) % length) for i in range(length)]
+    backward = [(i, (i - 1) % length) for i in range(length)]
+    out = jnp.zeros((*x.shape[:dim], length * rows, *x.shape[dim + 1 :]), x.dtype)
+    out = lax.dynamic_update_slice_in_dim(out, x, mine * rows, axis=dim)
+    from_left = from_right = x
+    middle = length // 2
+    for lap in range(1, middle + 1):
+        from_left = lax.ppermute(from_left, axis, right)
+        out = lax.dynamic_update_slice_in_dim(
+            out, from_left, (mine - lap) % length * rows, axis=dim
+        )
+        if lap < length - middle:
+            from_right = lax.ppermute(from_right, axis, backward)
+            out = lax.dynamic_update_slice_in_dim(
+                out, from_right, (mine + lap) % length * rows, axis=dim
+            )
+    return out
 
 
 def slot_numbers(route_rows, experts, capacity):
@@ -78,7 +99,7 @@
         .reshape(layout)
     )
     full_in, full_down = (
-        lax.all_gather(w_in, "dp", axis=1, tiled=True),
+        ring_gather(w_in, "dp", 1),
         lax.all_gather(w_down, "dp", axis=1, tiled=True),
     )
     inputs_here = lax.all_to_all(send_inputs, "expert", split_axis=0, concat_axis=0, tiled=True)

time: 372 us -> 371 us (level)
  waiting for transfers between devices: 229 us -> 190 us
  starting transfers between devices: 37.9 us -> 60 us
  local copies, waits for them, and re-layouts: 29.8 us -> 42.8 us
    all_to_all x1, waiting for transfers between devices: 40.7 us -> 13 us  [body(): lax.all_to_all(send_inputs, 'expert', split_axis=0, concat_axis=0, tiled=...]
    all_gather x1 -> x0, waiting for transfers between devices: 26.6 us -> none  [body(): lax.all_gather(w_in, 'dp', axis=1, tiled=True)]
    ppermute x0 -> x15, starting transfers between devices: none -> 24.9 us  [the longest x8 24.9 us: ring_gather(): from_left = lax.ppermute(from_left, axis, right)]
    dynamic_update_slice x0 -> x16, local copies, waits for them, and re-layouts: none -> 13 us  [the longest x8 6.97 us: ring_gather(): lax.dynamic_update_slice_in_dim(out, from_left, (mine - lap) % length * r...]
    all_to_all x1, waiting for transfers between devices: 0.01 us -> 9.23 us  [body(): lax.all_to_all(send_grads, 'expert', split_axis=0, concat_axis=0, tiled=T...]
    unnamed x5 -> x4, waiting for transfers between devices: 125 us -> 128 us
    unnamed x28 -> x24, local copies, waits for them, and re-layouts: 8.68 us -> 7.5 us
  transfers between devices with their start and end apart: 7 -> 21, of which waited for: 5 -> 10; matrix products, arithmetic and copies ran while one was open for 11% -> 16% of each run, Pallas kernels for 0% -> 0%
where the time goes in v1:
time: 371 us; the launch traced here: 370 us
  waiting for transfers between devices  190 us (51%)
  starting transfers between devices  60 us (16%)
  local copies, waits for them, and re-layouts  42.8 us (12%)
  matrix products  27.8 us (7%)
  blocking collectives  18.4 us (5%)
  other arithmetic  15.9 us (4%)
  between operations  15 us (4%)
    unnamed x4, waiting for transfers between devices  128 us
    all_to_all x1, waiting for transfers between devices, body(): lax.all_to_all(grad_inputs, 'expert', split_axis=0, concat_axis=0, tiled=...  36.1 us
    ppermute x8, starting transfers between devices, ring_gather(): from_left = lax.ppermute(from_left, axis, right)  24.9 us
    all_gather x1, blocking collectives, body(): lax.all_gather(w_down, 'dp', axis=1, tiled=True)  18.4 us
    all_to_all x1, starting transfers between devices, body(): lax.all_to_all(send_inputs, 'expert', split_axis=0, concat_axis=0, tiled=...  13 us
    all_to_all x1, waiting for transfers between devices, body(): lax.all_to_all(send_inputs, 'expert', split_axis=0, concat_axis=0, tiled=...  13 us
    all_to_all x1, waiting for transfers between devices, body(): lax.all_to_all(send_grads, 'expert', split_axis=0, concat_axis=0, tiled=T...  9.23 us
    scatter x1, other arithmetic, body(): send_grads = jnp.zeros((experts * capacity, model_width), jnp.bfloat16).a...  8.61 us
  transfers between devices with their start and end apart: 21, of which 10 were waited for; matrix products, arithmetic and copies ran while one was open for 16% of the time, Pallas kernels for 0%

profile of v1, /device:TPU:25, one launch (start us, length us, event | category | flops | bytes accessed | tf_op | source)
XLA Modules:
  0.0 370.2 jit_solution(11377547816620565146)
XLA Ops:
  7.2 0.8 copy.34
  8.2 0.7 broadcast_multiply_fusion
  8.9 1.2 reduce-window.6
  10.7 7.7 %scatter_custom_fusion = bf16[1024,1024]{1,0:T(8,128)(2,1)} fusion(s32[512]{0:T(512)S(1)} %bitcast.173, bf16[128,1024]{1,0:T(8,128)(2,1)S(1)} %copy-done, s32[1024]{0:T(1024)S(1)} %pad_clamp_fusion.1, bf16[]{:T(256)} %constant.143.clone.1), kind=kCustom, calls=%fused_computation.41 | custom fusion | bytes 2097154 | tf_op jit(solution)/shard_map/scatter | solution.py:89
  18.5 13.0 %all-to-all-start = ((bf16[32,1,32,1024]{3,2,1,0:T(8,128)(2,1)}), bf16[32,1,32,1024]{3,2,1,0:T(8,128)(2,1)S(1)}, u32[]{:S(2)}, u32[]{:S(2)}) async-start(bf16[32,1,32,1024]{3,2,1,0:T(8,128)(2,1)} %bitcast.21), calls=%async_computation | async-start | bytes 4194304 | tf_op jit(solution)/shard_map/all_to_all | solution.py:105
  31.5 3.4 collective-permute-start
  34.9 18.4 %all_gather.3 = bf16[1,384,1024]{2,1,0:T(8,128)(2,1)S(1)} all-gather(bf16[1,24,1024]{2,1,0:T(8,128)(2,1)S(1)} %copy-done.3), channel_id=1, replica_groups=mesh['dp'=16,'expert'=32] {'dp'}, dimensions={1}, use_global_device_ids=true | all-gather | bytes 835584 | tf_op jit(solution)/shard_map/all_gather | solution.py:103
  53.3 1.3 broadcast.193
  54.6 0.6 bitcast_dynamic-update-slice_fusion.15
  55.5 8.6 %scatter_custom_fusion.1 = bf16[1024,1024]{1,0:T(8,128)(2,1)} fusion(s32[512]{0:T(512)S(1)} %bitcast.174, f32[512]{0:T(512)S(1)} %mul.232, bf16[]{:T(256)} %constant.143.clone.1, bf16[128,1024]{1,0:T(8,128)(2,1)} %param.11, s32[1024]{0:T(1024)S(1)} %pad_clamp_fusion.1), kind=kCustom, calls=%fused_computation.40 | custom fusion | flops 1572864 | bytes 2365442 | tf_op jit(solution)/shard_map/scatter | solution.py:98
  64.1 1.7 collective-permute-start.2
  65.9 1.6 bitcast_dynamic-update-slice_fusion.14
  67.4 13.0 %all-to-all-done = bf16[32,1,32,1024]{3,2,1,0:T(8,128)(2,1)S(1)} async-done(((bf16[32,1,32,1024]{3,2,1,0:T(8,128)(2,1)}), bf16[32,1,32,1024]{3,2,1,0:T(8,128)(2,1)S(1)}, u32[]{:S(2)}, u32[]{:S(2)}) %all-to-all-start) | async-done | bytes 2097184 | tf_op jit(solution)/shard_map/all_to_all | solution.py:105
  80.4 7.4 %all-to-all-start.2 = ((bf16[32,1,32,1024]{3,2,1,0:T(8,128)(2,1)}), bf16[32,1,32,1024]{3,2,1,0:T(8,128)(2,1)}, u32[]{:S(2)}, u32[]{:S(2)}) async-start(bf16[32,1,32,1024]{3,2,1,0:T(8,128)(2,1)} %bitcast.34), calls=%async_computation.2 | async-start | bytes 4194304 | tf_op jit(solution)/shard_map/all_to_all | solution.py:108
  87.8 0.6 bitcast_dynamic-update-slice_fusion.13
  88.4 3.6 collective-permute-start.4
  92.0 1.6 bitcast_dynamic-update-slice_fusion.12
  93.6 1.5 bitcast_dynamic-update-slice_fusion.11
  95.1 2.9 collective-permute-start.6
  98.1 0.6 bitcast_dynamic-update-slice_fusion.10
  98.7 0.6 bitcast_dynamic-update-slice_fusion.9
  99.3 0.4 collective-permute-done.6
  99.7 3.6 collective-permute-start.8
  103.3 0.4 collective-permute-done.7
  103.7 0.6 bitcast_dynamic-update-slice_fusion.8
  104.3 0.6 bitcast_dynamic-update-slice_fusion.7
  105.0 3.6 collective-permute-start.10
  108.6 0.8 collective-permute-done.9
  109.4 0.6 bitcast_dynamic-update-slice_fusion.6
  110.0 0.6 bitcast_dynamic-update-slice_fusion.5
  110.6 3.2 collective-permute-start.12
  113.8 1.2 collective-permute-done.11
  115.0 0.6 bitcast_dynamic-update-slice_fusion.4
  115.7 0.6 bitcast_dynamic-update-slice_fusion.3
  116.3 3.0 collective-permute-start.14
  119.3 0.6 bitcast_dynamic-update-slice_fusion.2
  119.9 0.8 collective-permute-done.13
  120.7 0.6 bitcast_dynamic-update-slice_fusion.1
  121.3 0.7 bitcast_dynamic-update-slice_fusion
  122.0 5.0 %multiply_bitcast_fusion = f32[32,1,32,768]{3,2,0,1:T(8,128)} fusion(bf16[32,1,32,1024]{3,2,1,0:T(8,128)(2,1)S(1)} %all-to-all-done, bf16[1024,768]{1,0:T(8,128)(2,1)} %bitcast_dynamic-update-slice_fusion), kind=kOutput, calls=%fused_computation.10 | convolution fusion | flops 1611399168 | bytes 6815744 | tf_op jit(solution)/shard_map/sxcd,xdj->sxcj/dot_general | solution.py:43
  126.9 9.2 %all-to-all-done.2 = bf16[32,1,32,1024]{3,2,1,0:T(8,128)(2,1)} async-done(((bf16[32,1,32,1024]{3,2,1,0:T(8,128)(2,1)}), bf16[32,1,32,1024]{3,2,1,0:T(8,128)(2,1)}, u32[]{:S(2)}, u32[]{:S(2)}) %all-to-all-start.2) | async-done | bytes 2097184 | tf_op jit(solution)/shard_map/all_to_all | solution.py:108
  136.2 5.2 %fusion.44 = (bf16[32,32,384]{2,1,0:T(8,128)(2,1)S(1)}, bf16[32,32,384]{2,1,0:T(8,128)(2,1)S(1)}, bf16[32,32,384]{2,1,0:T(8,128)(2,1)}) fusion(f32[32,1,32,768]{3,2,0,1:T(8,128)} %multiply_bitcast_fusion, bf16[1,384,1024]{2,1,0:T(8,128)(2,1)S(1)} %all_gather.3, bf16[32,1,32,1024]{3,2,1,0:T(8,128)(2,1)} %all-to-all-done.2), kind=kOutput, calls=%fused_computation.50 | convolution fusion | flops 811597824 | bytes 8388608 | tf_op jit(solution)/shard_map/sxcd,xfd->sxcf/dot_general | solution.py:59
  141.4 5.2 %fusion.1 = bf16[32,1,32,1024]{3,2,1,0:T(8,128)(2,1)} fusion(bf16[1024,768]{1,0:T(8,128)(2,1)} %bitcast_dynamic-update-slice_fusion, bf16[32,32,384]{2,1,0:T(8,128)(2,1)S(1)} %get-tuple-element.17, bf16[32,32,384]{2,1,0:T(8,128)(2,1)S(1)} %get-tuple-element.16), kind=kOutput, calls=%fused_computation.11 | convolution fusion | flops 1615855616 | bytes 5242880 | tf_op jit(solution)/shard_map/sxcj,xdj->sxcd/dot_general | solution.py:69
  146.6 7.1 %all-to-all-start.3 = ((bf16[32,1,32,1024]{3,2,1,0:T(8,128)(2,1)}), bf16[32,1,32,1024]{3,2,1,0:T(8,128)(2,1)S(1)}, u32[]{:S(2)}, u32[]{:S(2)}) async-start(bf16[32,1,32,1024]{3,2,1,0:T(8,128)(2,1)} %fusion.1), calls=%async_computation.3 | async-start | bytes 4194304 | tf_op jit(solution)/shard_map/all_to_all | solution.py:110
  153.7 3.9 %fusion.31 = bf16[384,1,1024]{0,2,1:T(8,128)(2,1)} fusion(bf16[32,32,384]{2,1,0:T(8,128)(2,1)} %get-tuple-element.18, bf16[32,1,32,1024]{3,2,1,0:T(8,128)(2,1)} %all-to-all-done.2), kind=kOutput, calls=%fused_computation.39 | convolution fusion | flops 806092800 | bytes 3670016 | tf_op jit(solution)/shard_map/sxcf,sxcd->fxd/dot_general | solution.py:133
  157.7 4.8 %copy.43 = bf16[384,1,1024]{2,1,0:T(2,128)(2,1)} copy(bf16[384,1,1024]{0,2,1:T(8,128)(2,1)} %fusion.31) | data formatting | bytes 1572864 | tf_op jit(solution)/shard_map/convert_element_type | solution.py:135
  162.5 3.7 %fusion.14 = bf16[32,1,32,1024]{3,2,1,0:T(8,128)(2,1)} fusion(bf16[32,32,384]{2,1,0:T(8,128)(2,1)} %get-tuple-element.18, bf16[1,384,1024]{2,1,0:T(8,128)(2,1)S(1)} %all_gather.3), kind=kOutput, calls=%fused_computation.22 | convolution fusion | flops 807403520 | bytes 3670016 | tf_op jit(solution)/shard_map/sxcf,xfd->sxcd/dot_general | solution.py:50
  166.2 36.1 %all-to-all-done.3 = bf16[32,1,32,1024]{3,2,1,0:T(8,128)(2,1)S(1)} async-done(((bf16[32,1,32,1024]{3,2,1,0:T(8,128)(2,1)}), bf16[32,1,32,1024]{3,2,1,0:T(8,128)(2,1)S(1)}, u32[]{:S(2)}, u32[]{:S(2)}) %all-to-all-start.3) | async-done | bytes 2097184 | tf_op jit(solution)/shard_map/all_to_all | solution.py:110
  202.3 7.2 %all-to-all-start.1 = ((bf16[32,1,32,1024]{3,2,1,0:T(8,128)(2,1)}), bf16[32,1,32,1024]{3,2,1,0:T(8,128)(2,1)}, u32[]{:S(2)}, u32[]{:S(2)}) async-start(bf16[32,1,32,1024]{3,2,1,0:T(8,128)(2,1)} %fusion.14), calls=%async_computation.1 | async-start | bytes 4194304 | tf_op jit(solution)/shard_map/all_to_all | solution.py:107
  209.9 4.8 %fusion.23 = bf16[1024,768]{0,1:T(8,128)(2,1)} fusion(bf16[32,1,32,1024]{3,2,1,0:T(8,128)(2,1)} %copy-done.1, bf16[32,32,384]{2,1,0:T(8,128)(2,1)} %copy-done.7, bf16[32,32,384]{2,1,0:T(8,128)(2,1)S(1)} %copy-done.6), kind=kOutput, calls=%fused_computation.37 | convolution fusion | flops 1615331328 | bytes 5242880 | tf_op jit(solution)/shard_map/sxcd,sxcj->dxj/dot_general | solution.py:121
  214.7 2.6 copy.48
  217.5 1.3 dynamic-slice
  219.4 66.2 %all-reduce.3.cloned.1.call-done = bf16[384,1,1024]{2,1,0:T(2,128)(2,1)} async-done(((bf16[384,1,1024]{2,1,0:T(2,128)(2,1)}), bf16[384,1,1024]{2,1,0:T(2,128)(2,1)}) %all-reduce.3.cloned.1.call-update) | async-done | bytes 786448
  285.6 1.0 fusion.49
  286.7 0.6 copy.45
  287.3 62.2 %reduce-scatter.4.cloned.1.call-done = bf16[64,768]{1,0:T(8,128)(2,1)} async-done(((bf16[1024,768]{1,0:T(8,128)(2,1)}), bf16[64,768]{1,0:T(8,128)(2,1)}) %reduce-scatter.4.cloned.1.call-update) | async-done | bytes 98320
  349.5 1.1 copy.49
  350.6 0.8 copy.44
  351.4 2.0 gather_fusion.1
  353.5 0.4 gather.18
  353.9 2.1 reduce_sum.32
  356.0 4.6 %gather_fusion = bf16[512,1024]{1,0:T(8,128)(2,1)S(1)} fusion(bf16[1024,1024]{1,0:T(8,128)(2,1)} %bitcast.33, s32[1024]{0:T(1024)S(1)} %pad_clamp_fusion), kind=kCustom, calls=%fused_computation.1 | custom fusion | bytes 2099200 | tf_op jit(solution)/shard_map/gather | solution.py:111
  360.6 0.7 reshape.296
  361.3 2.1 multiply_reduce_fusion
  (55 shorter events, 1.7 us)
Async XLA Ops:
  7.2 3.6 copy-start
  18.5 13.0 %copy-start.2 = (bf16[1,64,768]{2,1,0:T(8,128)(2,1)S(1)}, bf16[1,64,768]{2,1,0:T(8,128)(2,1)}, u32[]{:S(2)}) copy-start(bf16[1,64,768]{2,1,0:T(8,128)(2,1)} %param.9) | copy-start | bytes 294916
  18.5 16.4 %copy-start.3 = (bf16[1,24,1024]{2,1,0:T(8,128)(2,1)S(1)}, bf16[1,24,1024]{2,1,0:T(8,128)(2,1)}, u32[]{:S(2)}) copy-start(bf16[1,24,1024]{2,1,0:T(8,128)(2,1)} %param.10) | copy-start | bytes 147460
  18.5 61.9 %all-to-all-start = ((bf16[32,1,32,1024]{3,2,1,0:T(8,128)(2,1)}), bf16[32,1,32,1024]{3,2,1,0:T(8,128)(2,1)S(1)}, u32[]{:S(2)}, u32[]{:S(2)}) async-start(bf16[32,1,32,1024]{3,2,1,0:T(8,128)(2,1)} %bitcast.21), calls=%async_computation | async-start | bytes 4194304 | tf_op jit(solution)/shard_map/all_to_all | solution.py:105
  31.5 23.7 %copy-start.4 = (f32[128,4]{0,1:T(4,128)S(1)}, f32[128,4]{0,1:T(4,128)}, u32[]{:S(2)}) copy-start(f32[128,4]{0,1:T(4,128)} %param.8) | copy-start | bytes 6148
  31.5 32.6 %collective-permute-start = (bf16[1,64,768]{2,1,0:T(8,128)(2,1)S(1)}, bf16[1,64,768]{2,1,0:T(8,128)(2,1)}, u32[]{:S(2)}, u32[]{:S(2)}) collective-permute-start(bf16[1,64,768]{2,1,0:T(8,128)(2,1)S(1)} %copy-done.2), channel_id=1, source_target_pairs={{0,32},{32,64},{64,96},{96,128},{128,160},{160,192},{192,224},{224... | collective-permute-start | bytes 294920 | tf_op jit(solution)/shard_map/ppermute | solution.py:18
  34.9 31.0 %collective-permute-start.1 = (bf16[1,64,768]{2,1,0:T(8,128)(2,1)S(1)}, bf16[1,64,768]{2,1,0:T(8,128)(2,1)S(1)}, u32[]{:S(2)}, u32[]{:S(2)}) collective-permute-start(bf16[1,64,768]{2,1,0:T(8,128)(2,1)S(1)} %copy-done.2), channel_id=1, source_target_pairs={{0,480},{32,0},{64,32},{96,64},{128,96},{160,128},{192,160},{224,1... | collective-permute-start | bytes 294920 | tf_op jit(solution)/shard_map/ppermute | solution.py:23
  64.1 24.3 %collective-permute-start.2 = (bf16[1,64,768]{2,1,0:T(8,128)(2,1)}, bf16[1,64,768]{2,1,0:T(8,128)(2,1)}, u32[]{:S(2)}, u32[]{:S(2)}) collective-permute-start(bf16[1,64,768]{2,1,0:T(8,128)(2,1)} %collective-permute-done), channel_id=1, source_target_pairs={{0,32},{32,64},{64,96},{96,128},{128,160},{160,192},{192,224},{224... | collective-permute-start | bytes 294920 | tf_op jit(solution)/shard_map/ppermute | solution.py:18
  65.9 26.2 %collective-permute-start.3 = (bf16[1,64,768]{2,1,0:T(8,128)(2,1)S(1)}, bf16[1,64,768]{2,1,0:T(8,128)(2,1)}, u32[]{:S(2)}, u32[]{:S(2)}) collective-permute-start(bf16[1,64,768]{2,1,0:T(8,128)(2,1)S(1)} %collective-permute-done.1), channel_id=1, source_target_pairs={{0,480},{32,0},{64,32},{96,64},{128,96},{160,128},{192,160},{224,1... | collective-permute-start | bytes 294920 | tf_op jit(solution)/shard_map/ppermute | solution.py:23
  80.4 41.6 %copy-start.1 = (bf16[32,1,32,1024]{3,2,1,0:T(8,128)(2,1)}, bf16[32,1,32,1024]{3,2,1,0:T(8,128)(2,1)S(1)}, u32[]{:S(2)}) copy-start(bf16[32,1,32,1024]{3,2,1,0:T(8,128)(2,1)S(1)} %all-to-all-done) | copy-start | bytes 6291460
  80.4 55.8 %all-to-all-start.2 = ((bf16[32,1,32,1024]{3,2,1,0:T(8,128)(2,1)}), bf16[32,1,32,1024]{3,2,1,0:T(8,128)(2,1)}, u32[]{:S(2)}, u32[]{:S(2)}) async-start(bf16[32,1,32,1024]{3,2,1,0:T(8,128)(2,1)} %bitcast.34), calls=%async_computation.2 | async-start | bytes 4194304 | tf_op jit(solution)/shard_map/all_to_all | solution.py:108
  88.4 6.7 %collective-permute-start.4 = (bf16[1,64,768]{2,1,0:T(8,128)(2,1)}, bf16[1,64,768]{2,1,0:T(8,128)(2,1)S(1)}, u32[]{:S(2)}, u32[]{:S(2)}) collective-permute-start(bf16[1,64,768]{2,1,0:T(8,128)(2,1)} %collective-permute-done.2), channel_id=1, source_target_pairs={{0,32},{32,64},{64,96},{96,128},{128,160},{160,192},{192,224},{224... | collective-permute-start | bytes 294920 | tf_op jit(solution)/shard_map/ppermute | solution.py:18
  92.0 6.0 %collective-permute-start.5 = (bf16[1,64,768]{2,1,0:T(8,128)(2,1)}, bf16[1,64,768]{2,1,0:T(8,128)(2,1)S(1)}, u32[]{:S(2)}, u32[]{:S(2)}) collective-permute-start(bf16[1,64,768]{2,1,0:T(8,128)(2,1)} %collective-permute-done.3), channel_id=1, source_target_pairs={{0,480},{32,0},{64,32},{96,64},{128,96},{160,128},{192,160},{224,1... | collective-permute-start | bytes 294920 | tf_op jit(solution)/shard_map/ppermute | solution.py:23
  95.1 4.6 %collective-permute-start.6 = (bf16[1,64,768]{2,1,0:T(8,128)(2,1)S(1)}, bf16[1,64,768]{2,1,0:T(8,128)(2,1)S(1)}, u32[]{:S(2)}, u32[]{:S(2)}) collective-permute-start(bf16[1,64,768]{2,1,0:T(8,128)(2,1)S(1)} %collective-permute-done.4), channel_id=1, source_target_pairs={{0,32},{32,64},{64,96},{96,128},{128,160},{160,192},{192,224},{224... | collective-permute-start | bytes 294920 | tf_op jit(solution)/shard_map/ppermute | solution.py:18
  98.1 5.7 %collective-permute-start.7 = (bf16[1,64,768]{2,1,0:T(8,128)(2,1)S(1)}, bf16[1,64,768]{2,1,0:T(8,128)(2,1)S(1)}, u32[]{:S(2)}, u32[]{:S(2)}) collective-permute-start(bf16[1,64,768]{2,1,0:T(8,128)(2,1)S(1)} %collective-permute-done.5), channel_id=1, source_target_pairs={{0,480},{32,0},{64,32},{96,64},{128,96},{160,128},{192,160},{224,1... | collective-permute-start | bytes 294920 | tf_op jit(solution)/shard_map/ppermute | solution.py:23
  99.7 5.3 %collective-permute-start.8 = (bf16[1,64,768]{2,1,0:T(8,128)(2,1)S(1)}, bf16[1,64,768]{2,1,0:T(8,128)(2,1)S(1)}, u32[]{:S(2)}, u32[]{:S(2)}) collective-permute-start(bf16[1,64,768]{2,1,0:T(8,128)(2,1)S(1)} %collective-permute-done.6), channel_id=1, source_target_pairs={{0,32},{32,64},{64,96},{96,128},{128,160},{160,192},{192,224},{224... | collective-permute-start | bytes 294920 | tf_op jit(solution)/shard_map/ppermute | solution.py:18
  103.7 5.7 %collective-permute-start.9 = (bf16[1,64,768]{2,1,0:T(8,128)(2,1)S(1)}, bf16[1,64,768]{2,1,0:T(8,128)(2,1)S(1)}, u32[]{:S(2)}, u32[]{:S(2)}) collective-permute-start(bf16[1,64,768]{2,1,0:T(8,128)(2,1)S(1)} %collective-permute-done.7), channel_id=1, source_target_pairs={{0,480},{32,0},{64,32},{96,64},{128,96},{160,128},{192,160},{224,1... | collective-permute-start | bytes 294920 | tf_op jit(solution)/shard_map/ppermute | solution.py:23
  105.0 5.7 %collective-permute-start.10 = (bf16[1,64,768]{2,1,0:T(8,128)(2,1)S(1)}, bf16[1,64,768]{2,1,0:T(8,128)(2,1)S(1)}, u32[]{:S(2)}, u32[]{:S(2)}) collective-permute-start(bf16[1,64,768]{2,1,0:T(8,128)(2,1)S(1)} %collective-permute-done.8), channel_id=1, source_target_pairs={{0,32},{32,64},{64,96},{96,128},{128,160},{160,192},{192,224},{224... | collective-permute-start | bytes 294920 | tf_op jit(solution)/shard_map/ppermute | solution.py:18
  109.4 5.7 %collective-permute-start.11 = (bf16[1,64,768]{2,1,0:T(8,128)(2,1)S(1)}, bf16[1,64,768]{2,1,0:T(8,128)(2,1)S(1)}, u32[]{:S(2)}, u32[]{:S(2)}) collective-permute-start(bf16[1,64,768]{2,1,0:T(8,128)(2,1)S(1)} %collective-permute-done.9), channel_id=1, source_target_pairs={{0,480},{32,0},{64,32},{96,64},{128,96},{160,128},{192,160},{224,1... | collective-permute-start | bytes 294920 | tf_op jit(solution)/shard_map/ppermute | solution.py:23
  110.6 5.7 %collective-permute-start.12 = (bf16[1,64,768]{2,1,0:T(8,128)(2,1)S(1)}, bf16[1,64,768]{2,1,0:T(8,128)(2,1)S(1)}, u32[]{:S(2)}, u32[]{:S(2)}) collective-permute-start(bf16[1,64,768]{2,1,0:T(8,128)(2,1)S(1)} %collective-permute-done.10), channel_id=1, source_target_pairs={{0,32},{32,64},{64,96},{96,128},{128,160},{160,192},{192,224},{224... | collective-permute-start | bytes 294920 | tf_op jit(solution)/shard_map/ppermute | solution.py:18
  115.0 5.7 %collective-permute-start.13 = (bf16[1,64,768]{2,1,0:T(8,128)(2,1)S(1)}, bf16[1,64,768]{2,1,0:T(8,128)(2,1)S(1)}, u32[]{:S(2)}, u32[]{:S(2)}) collective-permute-start(bf16[1,64,768]{2,1,0:T(8,128)(2,1)S(1)} %collective-permute-done.11), channel_id=1, source_target_pairs={{0,480},{32,0},{64,32},{96,64},{128,96},{160,128},{192,160},{224,1... | collective-permute-start | bytes 294920 | tf_op jit(solution)/shard_map/ppermute | solution.py:23
  116.3 5.0 %collective-permute-start.14 = (bf16[1,64,768]{2,1,0:T(8,128)(2,1)S(1)}, bf16[1,64,768]{2,1,0:T(8,128)(2,1)S(1)}, u32[]{:S(2)}, u32[]{:S(2)}) collective-permute-start(bf16[1,64,768]{2,1,0:T(8,128)(2,1)S(1)} %collective-permute-done.12), channel_id=1, source_target_pairs={{0,32},{32,64},{64,96},{96,128},{128,160},{160,192},{192,224},{224... | collective-permute-start | bytes 294920 | tf_op jit(solution)/shard_map/ppermute | solution.py:18
  141.4 5.2 %copy-start.5 = (bf16[32,32,384]{2,1,0:T(8,128)(2,1)}, bf16[32,32,384]{2,1,0:T(8,128)(2,1)S(1)}, u32[]{:S(2)}) copy-start(bf16[32,32,384]{2,1,0:T(8,128)(2,1)S(1)} %get-tuple-element.16) | copy-start | bytes 2359300
  141.4 5.2 %copy-start.7 = (bf16[32,32,384]{2,1,0:T(8,128)(2,1)}, bf16[32,32,384]{2,1,0:T(8,128)(2,1)S(1)}, u32[]{:S(2)}) copy-start(bf16[32,32,384]{2,1,0:T(8,128)(2,1)S(1)} %get-tuple-element.17) | copy-start | bytes 2359300
  146.6 55.7 %all-to-all-start.3 = ((bf16[32,1,32,1024]{3,2,1,0:T(8,128)(2,1)}), bf16[32,1,32,1024]{3,2,1,0:T(8,128)(2,1)S(1)}, u32[]{:S(2)}, u32[]{:S(2)}) async-start(bf16[32,1,32,1024]{3,2,1,0:T(8,128)(2,1)} %fusion.1), calls=%async_computation.3 | async-start | bytes 4194304 | tf_op jit(solution)/shard_map/all_to_all | solution.py:110
  153.7 132.0 %all-reduce.3.cloned.1.call-start = ((), (), s32[]{:S(2)}) async-start(), calls=%async_computation.6 | async-start | bytes 3145728
  166.2 43.7 %copy-start.6 = (bf16[32,32,384]{2,1,0:T(8,128)(2,1)S(1)}, bf16[32,32,384]{2,1,0:T(8,128)(2,1)}, u32[]{:S(2)}) copy-start(bf16[32,32,384]{2,1,0:T(8,128)(2,1)} %copy-done.5) | copy-start | bytes 2359300
  202.3 153.7 %all-to-all-start.1 = ((bf16[32,1,32,1024]{3,2,1,0:T(8,128)(2,1)}), bf16[32,1,32,1024]{3,2,1,0:T(8,128)(2,1)}, u32[]{:S(2)}, u32[]{:S(2)}) async-start(bf16[32,1,32,1024]{3,2,1,0:T(8,128)(2,1)} %fusion.14), calls=%async_computation.1 | async-start | bytes 4194304 | tf_op jit(solution)/shard_map/all_to_all | solution.py:107
  209.5 140.0 %reduce-scatter.4.cloned.1.call-start = ((), (), s32[]{:S(2)}) async-start(), calls=%async_computation.5 | async-start | bytes 1671168
Sparse Core Ops, SparseCore 0:
  162.6 122.9 all-reduce.2
  288.7 60.7 reduce-scatter.3
